TPU v7x, 32 devices: a whole 2x2x4 slice. The times are simulated.
32 devices in a mesh: req: 16 (over z, x, core), kv: 2 (over y).
Axes of the slice: x: 2, y: 2, z: 4, core: 2. Of those that a mesh axis runs over, the one named last changes fastest.
Arguments:
- hidden: bfloat16 [32, 256, 1024], P('req', 'kv'), may hold values from -6 to 6
- queries: bfloat16 [32, 256, 1024], P('req', 'kv'), may hold values from -24 to 24
- span_kv: bfloat16 [32, 256, 8, 128], P('req', 'kv'), may hold values from -48 to 48
- cache: bfloat16 [32, 2048, 8, 128], P('req', 'kv'), may hold values from -48 to 48
- req_order: int32 [32], replicated, may hold values from 0 to 31, each once
- cached_len: int32 [32], replicated, may hold values from 8 to 2048, as said below
- out_weight: bfloat16 [1024, 1024], replicated, may hold values from -0.1875 to 0.1875
- norm_gain: float32 [1024], replicated, may hold values from 0.1 to 1.9
- expert_ids: int32 [8192, 8], P(('req', 'kv')), may hold values from 0 to 15, all different within a row; in each aligned block of 256 rows (0 to 255, 256 to 511, ...) at most 256 rows name the same one
- expert_weights: float32 [8192, 8], P(('req', 'kv')), may hold values from 0.05 to 0.5
- w_experts: bfloat16 [16, 3, 1024, 512], P('req', None, None, 'kv'), may hold values from -0.25 to 0.25
- block_map: int32 [32, 128], P('req'), may hold values from 0 to 4095, as said below
Outputs:
- layer_out: bfloat16 [32, 256, 1024], P('req', 'kv')
- decode_pool: bfloat16 [4096, 8, 16, 128], P('req', 'kv')
Inputs may be any that keep to these rules, and one draw needn't show every extreme that they name: `cached_len`: some request fills its cache. `block_map`: a permutation of the 4096 pool pages; pool page s belongs to req index s // 256; the pages that one kv index holds of the slots of one req index (positions of its cache share) go to every req index equally often. `expert_ids`: in the rows of one device no expert is named more than 256 times.
All inputs are finite; a program needn't handle non-finite values.
Results may differ from a plain program's by a relative error of at most 0.023.
Values may be sent and summed in bfloat16 or wider, within the bound.
No kernel may reach another device: no remote copies, remote signals or barrier semaphores. Data moves between devices by JAX's collectives and lax.ppermute only.
A program may use at most 128 MiB of HBM per device.

v0:
```python
import math
import jax
import jax.numpy as jnp
from jax import lax
from jax.sharding import PartitionSpec as P

BLOCK = 16


def lookup_lengths(req_order, cached_len, count):
    start = lax.axis_index("req") * count
    mine = lax.dynamic_slice_in_dim(req_order, start, count)
    match = mine[:, None] == jnp.arange(cached_len.shape[0], dtype=jnp.int32)[None, :]
    return jnp.sum(jnp.where(match, cached_len[None, :], 0), axis=1)


def score_block(query_rows, cache_rows, span_rows):
    span_count, group_count, width = query_rows.shape
    head_dim = cache_rows.shape[-1] // 2
    per_group = width // head_dim
    query_split = query_rows.reshape(span_count, group_count, per_group, head_dim)
    key_rows = jnp.concatenate([cache_rows[..., :head_dim], span_rows[..., :head_dim]], axis=0)
    value_rows = jnp.concatenate([cache_rows[..., head_dim:], span_rows[..., head_dim:]], axis=0)
    scores = jnp.einsum(
        "igsd,pgd->gsip", query_split, key_rows, preferred_element_type=jnp.float32
    ) * (1.0 / math.sqrt(head_dim))
    return (scores, value_rows)


def soft_weights(scores, allowed, value_rows):
    masked = jnp.where(allowed, scores, -1e30)
    row_max = jnp.max(masked, axis=-1, keepdims=True)
    probability = jnp.where(allowed, jnp.exp(masked - row_max), 0.0)
    prob_sum = jnp.sum(probability, axis=-1)
    weighted = jnp.einsum(
        "gsip,pgd->igsd",
        probability.astype(jnp.bfloat16),
        value_rows,
        preferred_element_type=jnp.float32,
    )
    return (weighted, jnp.transpose(row_max[..., 0], (2, 0, 1)), jnp.transpose(prob_sum, (2, 0, 1)))


def whole_request(operands):
    query_rows, cache_rows, span_rows, length = operands
    scores, value_rows = score_block(query_rows, cache_rows, span_rows)
    cached = cache_rows.shape[0]
    position = jnp.arange(scores.shape[-1])[None, :]
    query_pos = jnp.arange(query_rows.shape[0])[:, None]
    allowed = jnp.where(position < cached, position < length, position - cached <= query_pos)
    weighted, row_max, prob_sum = soft_weights(scores, allowed, value_rows)
    result = weighted / prob_sum[..., None]
    return result.reshape(query_rows.shape).astype(jnp.bfloat16)


def place_pages(page_rows, slot_numbers, slots_dev):
    owner_index = slot_numbers // slots_dev
    arrangement = jnp.argsort(owner_index, stable=True)
    return (page_rows[arrangement], (slot_numbers % slots_dev)[arrangement])


def body(
    hidden,
    queries,
    span_kv,
    cache,
    req_order,
    cached_len,
    out_weight,
    norm_gain,
    expert_ids,
    expert_weights,
    w_experts,
    block_map,
):
    local_reqs, local_tokens, width_model = hidden.shape
    row_count = local_reqs * local_tokens
    req_count = lax.axis_size("req")
    kv_count = lax.axis_size("kv")
    kv_heads = span_kv.shape[2]
    head_pair = span_kv.shape[3]
    group_width = queries.shape[2] // kv_heads
    group_count = kv_heads // kv_count
    slots_dev = local_reqs * block_map.shape[1]
    lengths = lookup_lengths(req_order, cached_len, local_reqs)
    queries_grouped = queries.reshape(local_reqs, local_tokens, kv_heads, group_width)
    cache_heads, span_heads, query_heads = (
        lax.all_to_all(cache, "kv", split_axis=2, concat_axis=1, tiled=True),
        lax.all_to_all(span_kv, "kv", split_axis=2, concat_axis=1, tiled=True),
        lax.all_to_all(queries_grouped, "kv", split_axis=2, concat_axis=1, tiled=True),
    )
    attn_heads = lax.map(whole_request, (query_heads, cache_heads, span_heads, lengths))
    attn = lax.all_to_all(attn_heads, "kv", split_axis=1, concat_axis=2, tiled=True).reshape(
        row_count, kv_heads * group_width
    )
    page_total = block_map.shape[1]
    visible = jnp.arange(cache_heads.shape[1])[None, :] < lengths[:, None]
    visible_cache = jnp.where(visible[:, :, None, None], cache_heads, jnp.zeros((), jnp.bfloat16))
    page_rows = (
        visible_cache.reshape(local_reqs, page_total, BLOCK, group_count, head_pair)
        .transpose(0, 1, 3, 2, 4)
        .reshape(local_reqs * page_total, group_count, BLOCK, head_pair)
    )
    sorted_pages, local_slot = place_pages(page_rows, block_map.reshape(-1), slots_dev)
    per_owner = sorted_pages.shape[0] // req_count
    outgoing = sorted_pages.reshape(req_count, per_owner, group_count, BLOCK, head_pair)
    arrived, where_to = (
        lax.all_to_all(outgoing, "req", split_axis=0, concat_axis=0, tiled=True),
        lax.all_to_all(
            local_slot.reshape(req_count, per_owner), "req", split_axis=0, concat_axis=0, tiled=True
        ),
    )
    decode_pool = (
        jnp.zeros((slots_dev, group_count, BLOCK, head_pair), jnp.bfloat16)
        .at[where_to.reshape(-1)]
        .set(arrived.reshape(-1, group_count, BLOCK, head_pair))
    )
    residual = hidden.reshape(row_count, width_model).astype(jnp.float32) + jnp.dot(
        attn, out_weight, preferred_element_type=jnp.float32
    )
    inverse_rms = lax.rsqrt(jnp.mean(residual * residual, axis=-1, keepdims=True) + 1e-05)
    normed = (residual * inverse_rms * norm_gain).astype(jnp.bfloat16)
    top_count = expert_ids.shape[1]
    exp_dev = w_experts.shape[0]
    experts = exp_dev * req_count
    capacity = min(row_count, 2 * row_count * top_count // experts)
    chosen = expert_ids.reshape(-1)
    onehot = (chosen[:, None] == jnp.arange(experts, dtype=jnp.int32)[None, :]).astype(jnp.int32)
    slot_rank = jnp.sum(onehot * (jnp.cumsum(onehot, axis=0) - 1), axis=1)
    target = chosen * capacity + slot_rank
    source_row = jnp.arange(chosen.shape[0]) // top_count
    buffer = (
        jnp.zeros((experts * capacity, width_model), jnp.bfloat16)
        .at[target]
        .set(normed[source_row])
        .reshape(experts, capacity, width_model)
    )
    full_weights = lax.all_gather(w_experts, "kv", axis=3, tiled=True)
    slot_block = lax.all_to_all(buffer, "req", split_axis=0, concat_axis=0, tiled=True)
    source_count = slot_block.shape[0] // exp_dev
    grouped = slot_block.reshape(source_count, exp_dev, slot_block.shape[1], width_model)
    gate_act = jnp.einsum(
        "sejd,edf->sejf", grouped, full_weights[:, 0], preferred_element_type=jnp.float32
    )
    up_act = jnp.einsum(
        "sejd,edf->sejf", grouped, full_weights[:, 1], preferred_element_type=jnp.float32
    )
    activated = (jax.nn.silu(gate_act) * up_act).astype(jnp.bfloat16)
    expert_out = jnp.einsum(
        "sejf,edf->sejd", activated, full_weights[:, 2], preferred_element_type=jnp.float32
    ).astype(jnp.bfloat16)
    returned = lax.all_to_all(
        expert_out.reshape(slot_block.shape), "req", split_axis=0, concat_axis=0, tiled=True
    )
    picked = returned.reshape(experts * capacity, width_model)[target].reshape(
        row_count, top_count, width_model
    )
    expert_sum = jnp.sum(expert_weights[..., None] * picked.astype(jnp.float32), axis=1)
    layer_out = (
        (residual + expert_sum).astype(jnp.bfloat16).reshape(local_reqs, local_tokens, width_model)
    )
    return (layer_out, decode_pool)


def solution(mesh):
    return jax.shard_map(
        body,
        mesh=mesh,
        in_specs=(
            P("req", "kv", None),
            P("req", "kv", None),
            P("req", "kv", None, None),
            P("req", "kv", None, None),
            P(),
            P(),
            P(),
            P(),
            P(("req", "kv"), None),
            P(("req", "kv"), None),
            P("req", None, None, "kv"),
            P("req", None),
        ),
        out_specs=(P("req", "kv", None), P("req", "kv", None, None)),
        check_vma=False,
    )
```

profile of v0, /device:TPU:11, one launch (start us, length us, event | category | flops | bytes accessed | tf_op | source)
XLA Modules:
  0.0 748.4 jit_solution(12969157909613193286)
XLA Ops:
  7.2 2.1 copy.81
  9.3 3.5 all-to-all-start.1
  14.9 5.2 all-to-all-done.1
  20.1 3.5 all-to-all-start.2
  24.0 5.0 copy.78
  30.1 5.6 all-to-all-start
  35.7 4.5 reduce-window.6
  41.8 3.2 sort.17
  48.8 2.2 all_to_all.74
  52.0 28.7 %all-to-all-done = bf16[2,1024,8,128]{3,1,0,2:T(8,128)(2,1)} async-done(((bf16[2,1024,8,128]{3,1,0,2:T(8,128)(2,1)}), bf16[2,1024,8,128]{3,1,0,2:T(8,128)(2,1)}, u32[]{:S(2)}, u32[]{:S(2)}) %all-to-all-start) | async-done | bytes 4194336 | tf_op jit(solution)/shard_map/all_to_all | solution.py:88
  80.7 4.6 copy.80
  85.3 104.1 %while.12 = (s32[]{:T(128)}, bf16[2,256,4,128]{3,2,0,1:T(4,128)(2,1)}, bf16[2,2048,4,128]{3,1,2,0:T(8,128)(2,1)}, bf16[2,256,4,128]{1,3,2,0:T(8,128)(2,1)}, s32[...) while((s32[]{:T(128)}, bf16[2,256,4,128]{3,2,0,1:T(4,128)(2,1)}, ...), condition=%wide.region_4.5_spmd, body=%wide.region_1.4_spmd.sunk | while | flops 1251877888 | bytes 80653984 | solution.py:92
  85.3 3.0 constant_dynamic-slice_fusion.5
  88.3 4.0 copy.115
  92.3 2.8 fusion.64
  97.6 9.2 %fusion.65 = f32[4,2304,256,2]{2,1,3,0:T(8,128)} fusion(bf16[256,4,2,64]{0,3,2,1:T(8,128)(2,1)S(1)} %bitcast.190, bf16[256,4,64]{0,2,1:T(8,128)(2,1)} %get-tuple-element.183, bf16[2048,4,64]{0,2,1:T(8,128)(2,1)} %get-tuple-element.184), kind=kOutput, calls=%fused_computation.24.clone.1 | convolution fusion | flops 606339072 | bytes 20316160 | tf_op jit(solution)/shard_map/while/body/eval_jaxpr/igsd,pgd->gsip/dot_general | solution.py:24
  108.7 2.7 fusion.66
  111.4 19.4 %fusion.67 = (f32[4,2,256]{2,1,0:T(2,128)S(1)}, bf16[4,2,256,2304]{2,3,1,0:T(8,128)(2,1)}) fusion(f32[4,2304,256,2]{2,1,3,0:T(8,128)} %fusion.65, pred[256,2304]{0,1:T(8,128)(4,1)} %fusion.66), kind=kOutput, calls=%fused_computation.99.clone.1 | output fusion | flops 37751040 | bytes 28909568 | tf_op jit(solution)/shard_map/while/body/eval_jaxpr/sub | solution.py:33
  130.9 5.5 fusion.68
  137.3 3.0 constant_dynamic-slice_fusion.5
  140.4 4.0 copy.115
  144.4 2.8 fusion.64
  149.7 9.2 %fusion.65 = f32[4,2304,256,2]{2,1,3,0:T(8,128)} fusion(bf16[256,4,2,64]{0,3,2,1:T(8,128)(2,1)S(1)} %bitcast.190, bf16[256,4,64]{0,2,1:T(8,128)(2,1)} %get-tuple-element.183, bf16[2048,4,64]{0,2,1:T(8,128)(2,1)} %get-tuple-element.184), kind=kOutput, calls=%fused_computation.24.clone.1 | convolution fusion | flops 606339072 | bytes 20316160 | tf_op jit(solution)/shard_map/while/body/eval_jaxpr/igsd,pgd->gsip/dot_general | solution.py:24
  160.8 2.7 fusion.66
  163.5 19.4 %fusion.67 = (f32[4,2,256]{2,1,0:T(2,128)S(1)}, bf16[4,2,256,2304]{2,3,1,0:T(8,128)(2,1)}) fusion(f32[4,2304,256,2]{2,1,3,0:T(8,128)} %fusion.65, pred[256,2304]{0,1:T(8,128)(4,1)} %fusion.66), kind=kOutput, calls=%fused_computation.99.clone.1 | output fusion | flops 37751040 | bytes 28909568 | tf_op jit(solution)/shard_map/while/body/eval_jaxpr/sub | solution.py:33
  182.9 5.5 fusion.68
  189.4 3.6 all-to-all-start.3
  193.1 1.9 gather_fusion.1
  196.4 2.0 all-to-all-done.3
  198.4 10.7 %all-to-all-start.6 = ((s32[16,1,16]{2,1,0:T(1,128)}), s32[16,1,16]{2,1,0:T(1,128)S(1)}, u32[]{:S(2)}, u32[]{:S(2)}) async-start(s32[16,1,16]{2,1,0:T(1,128)} %all_to_all.84), calls=%async_computation.6 | async-start | bytes 16384 | tf_op jit(solution)/shard_map/all_to_all | solution.py:109
  210.5 2.0 multiply_reduce_fusion
  213.5 33.0 %scatter_custom_fusion = bf16[4096,1024]{1,0:T(8,128)(2,1)} fusion(s32[2048]{0:T(1024)S(1)} %bitcast.205, bf16[256,1024]{1,0:T(8,128)(2,1)} %multiply_convert_fusion, s32[2048]{0:T(1024)S(1)} %broadcast_clamp_fusion.1, bf16[]{:T(256)} %constant.114.clone.1), kind=kCustom, calls=%fused_computation.49 | custom fusion | bytes 8389120 | tf_op jit(solution)/shard_map/scatter | solution.py:135
  246.4 6.4 all-to-all-start.4
  253.5 2.6 select_bitcast_fusion
  256.1 3.3 copy.96
  259.4 5.2 gather_fusion.2
  264.6 170.4 %all-to-all-done.4 = bf16[16,256,1024]{2,1,0:T(8,128)(2,1)} async-done(((bf16[16,256,1024]{2,1,0:T(8,128)(2,1)}), bf16[16,256,1024]{2,1,0:T(8,128)(2,1)}, u32[]{:S(2)}, u32[]{:S(2)}) %all-to-all-start.4) | async-done | bytes 8388640 | tf_op jit(solution)/shard_map/all_to_all | solution.py:139
  435.0 4.9 all-to-all-start.7
  440.6 46.2 %all-gather.2.cloned.1.call-done = bf16[1,3,1024,512]{3,2,1,0:T(8,128)(2,1)} async-done(((bf16[1,3,1024,256]{3,2,1,0:T(8,128)(2,1)}), bf16[1,3,1024,512]{3,2,1,0:T(8,128)(2,1)}) %all-gather.2.cloned.1.call-update) | async-done | bytes 3145744 | tf_op jit(solution)/shard_map/all_gather | solution.py:138
  486.8 11.4 %fusion.38 = f32[16,256,512]{2,1,0:T(8,128)} fusion(bf16[16,256,1024]{2,1,0:T(8,128)(2,1)} %all-to-all-done.4, bf16[1,3,1024,512]{3,2,1,0:T(8,128)(2,1)} %all-gather.2.cloned.1.call-done), kind=kOutput, calls=%fused_computation.58 | convolution fusion | flops 4294967296 | bytes 17825792 | tf_op jit(solution)/shard_map/sejd,edf->sejf/dot_general | solution.py:142
  498.2 16.0 %convolution_convert_fusion = bf16[16,256,1024]{2,1,0:T(8,128)(2,1)} fusion(f32[16,256,512]{2,1,0:T(8,128)} %fusion.38, bf16[16,256,1024]{2,1,0:T(8,128)(2,1)} %all-to-all-done.4, bf16[1,3,1024,512]{3,2,1,0:T(8,128)(2,1)} %all-gather.2.cloned.1.call-done), kind=kOutput, calls=%fused_computation.47 | convolution fusion | flops 8606711808 | bytes 27262976 | tf_op jit(solution)/shard_map/sejf,edf->sejd/dot_general | solution.py:149
  514.2 18.2 %all-to-all-done.7 = bf16[16,16,4,16,128]{4,3,2,1,0:T(8,128)(2,1)} async-done(((bf16[16,16,4,16,128]{4,3,2,1,0:T(8,128)(2,1)}), bf16[16,16,4,16,128]{4,3,2,1,0:T(8,128)(2,1)}, u32[]{:S(2)}, u32[]{:S(2)}) %all-to-all-start.7) | async-done | bytes 4194336 | tf_op jit(solution)/shard_map/all_to_all | solution.py:108
  532.4 5.3 all-to-all-start.5
  539.1 3.1 broadcast_in_dim.106
  542.2 33.5 %scatter_fusion = bf16[256,4,16,128]{3,2,1,0:T(8,128)(2,1)} fusion(bf16[256,4,16,128]{3,2,1,0:T(8,128)(2,1)} %broadcast_in_dim.106, s32[256]{0:T(256)S(1)} %bitcast.209, bf16[256,4,16,128]{3,2,1,0:T(8,128)(2,1)} %bitcast.57), kind=kCustom, calls=%fused_computation.5 | custom fusion | bytes 12583936 | tf_op jit(solution)/shard_map/scatter | solution.py:116
  575.7 144.2 %all-to-all-done.5 = bf16[16,256,1024]{2,1,0:T(8,128)(2,1)} async-done(((bf16[16,256,1024]{2,1,0:T(8,128)(2,1)}), bf16[16,256,1024]{2,1,0:T(8,128)(2,1)}, u32[]{:S(2)}, u32[]{:S(2)}) %all-to-all-start.5) | async-done | bytes 8388640 | tf_op jit(solution)/shard_map/all_to_all | solution.py:152
  719.9 15.5 %gather_fusion = bf16[2048,1024]{1,0:T(8,128)(2,1)} fusion(bf16[4096,1024]{1,0:T(8,128)(2,1)} %bitcast.46, s32[2048]{0:T(1024)S(1)} %broadcast_clamp_fusion), kind=kCustom, calls=%fused_computation.1 | custom fusion | bytes 8396800 | tf_op jit(solution)/shard_map/gather | solution.py:155
  735.3 4.8 fusion.26
  (89 shorter events, 28.1 us)
Async XLA Ops:
  7.2 203.3 %copy-start = (bf16[1024,1024]{1,0:T(8,128)(2,1)S(1)}, bf16[1024,1024]{1,0:T(8,128)(2,1)}, u32[]{:S(2)}) copy-start(bf16[1024,1024]{1,0:T(8,128)(2,1)} %param.20) | copy-start | bytes 6291460
  7.2 16.5 %copy-start.4 = (s32[256,8]{0,1:T(8,128)S(1)}, s32[256,8]{0,1:T(8,128)}, u32[]{:S(2)}) copy-start(s32[256,8]{0,1:T(8,128)} %param.22) | copy-start | bytes 24580
  9.3 10.9 %all-to-all-start.1 = ((bf16[2,128,8,128]{3,1,0,2:T(8,128)(2,1)}), bf16[2,128,8,128]{3,1,0,2:T(8,128)(2,1)S(1)}, u32[]{:S(2)}, u32[]{:S(2)}) async-start(bf16[2,128,8,128]{3,1,0,2:T(8,128)(2,1)} %copy.81), calls=%async_computation.1 | async-start | bytes 1048576 | tf_op jit(solution)/shard_map/all_to_all | solution.py:89
  20.1 9.9 %all-to-all-start.2 = ((bf16[2,128,8,128]{1,3,0,2:T(8,128)(2,1)}), bf16[2,128,8,128]{1,3,0,2:T(8,128)(2,1)S(1)}, u32[]{:S(2)}, u32[]{:S(2)}) async-start(bf16[2,128,8,128]{1,3,0,2:T(8,128)(2,1)} %copy.84), calls=%async_computation.2 | async-start | bytes 1048576 | tf_op jit(solution)/shard_map/all_to_all | solution.py:90
  29.0 12.1 %copy-start.10 = (s32[32]{0:T(128)S(1)}, s32[32]{0:T(128)}, u32[]{:S(2)}) copy-start(s32[32]{0:T(128)} %param.18) | copy-start | bytes 388
  29.0 12.2 %copy-start.9 = (s32[2,128]{1,0:T(2,128)S(1)}, s32[2,128]{1,0:T(2,128)}, u32[]{:S(2)}) copy-start(s32[2,128]{1,0:T(2,128)} %param.25) | copy-start | bytes 3076
  29.0 16.0 %copy-start.11 = (s32[32]{0:T(128)S(1)}, s32[32]{0:T(128)}, u32[]{:S(2)}) copy-start(s32[32]{0:T(128)} %param.19) | copy-start | bytes 388
  30.1 50.6 %all-to-all-start = ((bf16[2,1024,8,128]{3,1,0,2:T(8,128)(2,1)}), bf16[2,1024,8,128]{3,1,0,2:T(8,128)(2,1)}, u32[]{:S(2)}, u32[]{:S(2)}) async-start(bf16[2,1024,8,128]{3,1,0,2:T(8,128)(2,1)} %copy.78), calls=%async_computation | async-start | bytes 8388608 | tf_op jit(solution)/shard_map/all_to_all | solution.py:88
  85.3 107.8 %copy-start.8 = (s32[256]{0:T(256)S(1)}, s32[256]{0:T(256)}, u32[]{:S(2)}) copy-start(s32[256]{0:T(256)} %compare_select_fusion.3) | copy-start | bytes 3076
  85.3 107.8 %copy-start.1 = (s32[256]{0:T(256)S(1)}, s32[256]{0:T(256)}, u32[]{:S(2)}) copy-start(s32[256]{0:T(256)} %get-tuple-element.133) | copy-start | bytes 3076
  92.3 2.8 copy-start.2
  92.3 3.5 copy-start.3
  144.4 2.8 copy-start.2
  144.4 3.5 copy-start.3
  189.4 23.1 %copy-start.7 = (f32[1024]{0:T(1024)S(1)}, f32[1024]{0:T(1024)}, u32[]{:S(2)}) copy-start(f32[1024]{0:T(1024)} %param.21) | copy-start | bytes 12292
  189.4 9.0 %all-to-all-start.3 = ((bf16[2,256,4,128]{3,2,0,1:T(4,128)(2,1)}), bf16[2,256,4,128]{3,2,0,1:T(4,128)(2,1)S(1)}, u32[]{:S(2)}, u32[]{:S(2)}) async-start(bf16[2,256,4,128]{3,2,0,1:T(4,128)(2,1)} %get-tuple-element.80), calls=%async_computation.3 | async-start | bytes 1048576 | tf_op jit(solution)/shard_map/all_to_all | solution.py:93
  195.0 18.4 %copy-start.5 = (s32[2048,1]{0,1:T(1,128)S(1)}, s32[2048,1]{0,1:T(1,128)}, u32[]{:S(2)}) copy-start(s32[2048,1]{0,1:T(1,128)} %compare_select_fusion.1) | copy-start | bytes 24580
  198.4 48.0 %all-to-all-start.6 = ((s32[16,1,16]{2,1,0:T(1,128)}), s32[16,1,16]{2,1,0:T(1,128)S(1)}, u32[]{:S(2)}, u32[]{:S(2)}) async-start(s32[16,1,16]{2,1,0:T(1,128)} %all_to_all.84), calls=%async_computation.6 | async-start | bytes 16384 | tf_op jit(solution)/shard_map/all_to_all | solution.py:109
  246.4 188.6 %all-to-all-start.4 = ((bf16[16,256,1024]{2,1,0:T(8,128)(2,1)}), bf16[16,256,1024]{2,1,0:T(8,128)(2,1)}, u32[]{:S(2)}, u32[]{:S(2)}) async-start(bf16[16,256,1024]{2,1,0:T(8,128)(2,1)} %bitcast.189), calls=%async_computation.4 | async-start | bytes 16777216 | tf_op jit(solution)/shard_map/all_to_all | solution.py:139
  435.0 97.4 %all-to-all-start.7 = ((bf16[16,16,4,16,128]{4,3,2,1,0:T(8,128)(2,1)}), bf16[16,16,4,16,128]{4,3,2,1,0:T(8,128)(2,1)}, u32[]{:S(2)}, u32[]{:S(2)}) async-start(bf16[16,16,4,16,128]{4,3,2,1,0:T(8,128)(2,1)} %bitcast.192), calls=%async_computation.7 | async-start | bytes 8388608 | tf_op jit(solution)/shard_map/all_to_all | solution.py:108
  439.9 46.9 %all-gather.2.cloned.1.call-start = ((), (), s32[]{:S(2)}) async-start(), calls=%async_computation.8 | async-start | bytes 4718592 | tf_op jit(solution)/shard_map/all_gather | solution.py:138
  514.2 23.5 %copy-start.6 = (f32[256,8]{0,1:T(8,128)S(1)}, f32[256,8]{0,1:T(8,128)}, u32[]{:S(2)}) copy-start(f32[256,8]{0,1:T(8,128)} %param.23) | copy-start | bytes 24580
  532.4 187.5 %all-to-all-start.5 = ((bf16[16,256,1024]{2,1,0:T(8,128)(2,1)}), bf16[16,256,1024]{2,1,0:T(8,128)(2,1)}, u32[]{:S(2)}, u32[]{:S(2)}) async-start(bf16[16,256,1024]{2,1,0:T(8,128)(2,1)} %convolution_convert_fusion), calls=%async_computation.5 | async-start | bytes 16777216 | tf_op jit(solution)/shard_map/all_to_all | solution.py:152
Sparse Core Ops, SparseCore 0:
  442.3 44.5 all-gather.1
where the time goes:
time: 760 us; the launch traced here: 748 us
  waiting for transfers between devices  417 us (55%)
  local copies, waits for them, and re-layouts  147 us (19%)
  other arithmetic  68.1 us (9%)
  matrix products  58.8 us (8%)
  starting transfers between devices  43.5 us (6%)
  between operations  14.8 us (2%)
    all_to_all x1, waiting for transfers between devices, body(): lax.all_to_all(buffer, 'req', split_axis=0, concat_axis=0, tiled=True)  170 us
    all_to_all x1, waiting for transfers between devices, body(): lax.all_to_all(expert_out.reshape(slot_block.shape), 'req', split_axis=0,...  144 us
    all_gather x1, waiting for transfers between devices, body(): full_weights = lax.all_gather(w_experts, 'kv', axis=3, tiled=True)  46.2 us
    sub x2, other arithmetic, soft_weights(): probability = jnp.where(allowed, jnp.exp(masked - row_max), 0.0)  38.9 us
    scatter x1, local copies, waits for them, and re-layouts, body(): decode_pool = jnp.zeros((slots_dev, group_count, BLOCK, head_pair), jnp.b...  33.5 us
    scatter x1, local copies, waits for them, and re-layouts, body(): buffer = jnp.zeros((experts * capacity, width_model), jnp.bfloat16).at[ta...  33 us
    all_to_all x1, waiting for transfers between devices, body(): lax.all_to_all(cache, 'kv', split_axis=2, concat_axis=1, tiled=True)  28.7 us
    dynamic_slice x10, local copies, waits for them, and re-layouts, body(): lax.map(whole_request, (query_heads, cache_heads, span_heads, lengths))  20.2 us
  transfers between devices with their start and end apart: 9, of which 8 were waited for; matrix products, arithmetic and copies ran while one was open for 19% of the time, Pallas kernels for 0%

commit v1 on v0

--- a/solution.py
+++ b/solution.py
@@ -1,3 +1,4 @@
+import functools
 import math
 import jax
 import jax.numpy as jnp
@@ -5,6 +6,29 @@
 from jax.sharding import PartitionSpec as P
 
 BLOCK = 16
+
+
+def state_cards_on_mesh(work_x, array_dim, axis_no):
+    tile_out, new = (lax.axis_size("req"), lax.axis_index("req"))
+    latest = work_x.shape[array_dim] // tile_out
+    block_out = list(work_x.shape)
+    block_out[array_dim] = latest
+    field_out = block_out[axis_no]
+    block_out[axis_no] = field_out * tile_out
+    wide_out = jnp.zeros(block_out, work_x.dtype)
+    for num in range(tile_out):
+        arr_out = lax.dynamic_slice_in_dim(work_x, (new ^ num) * latest, latest, axis=array_dim)
+        if num:
+            arr_out = lax.ppermute(
+                arr_out, axis_name="req", perm=list(map(lambda k: (k, k ^ num), range(tile_out)))
+            )
+        wide_out = lax.dynamic_update_slice_in_dim(
+            wide_out, arr_out, (new ^ num) * field_out, axis=axis_no
+        )
+    return wide_out
+
+
+_hold_face = functools.partial(state_cards_on_mesh, array_dim=0, axis_no=0)
 
 
 def lookup_lengths(req_order, cached_len, count):
@@ -105,7 +129,7 @@
     per_owner = sorted_pages.shape[0] // req_count
     outgoing = sorted_pages.reshape(req_count, per_owner, group_count, BLOCK, head_pair)
     arrived, where_to = (
-        lax.all_to_all(outgoing, "req", split_axis=0, concat_axis=0, tiled=True),
+        _hold_face(outgoing),
         lax.all_to_all(
             local_slot.reshape(req_count, per_owner), "req", split_axis=0, concat_axis=0, tiled=True
         ),

time: 760 us -> 817 us (1.075)
  starting transfers between devices: 43.5 us -> 70.9 us
  local copies, waits for them, and re-layouts: 147 us -> 165 us
  waiting for transfers between devices: 417 us -> 427 us
    ppermute x0 -> x15, waiting for transfers between devices: none -> 207 us  [state_cards_on_mesh(): lax.ppermute(arr_out, axis_name='req', perm=list(map(lambda k: (k, k ^ nu...]
    all_to_all x1, waiting for transfers between devices: 144 us -> 0.01 us  [body(): lax.all_to_all(expert_out.reshape(slot_block.shape), 'req', split_axis=0,...]
    all_gather x1, waiting for transfers between devices: 46.2 us -> 0.01 us  [body(): full_weights = lax.all_gather(w_experts, 'kv', axis=3, tiled=True)]
    ppermute x0 -> x15, starting transfers between devices: none -> 32.2 us  [state_cards_on_mesh(): lax.ppermute(arr_out, axis_name='req', perm=list(map(lambda k: (k, k ^ nu...]
    all_to_all x1 -> x0, waiting for transfers between devices: 18.2 us -> none  [body(): lax.all_to_all(outgoing, 'req', split_axis=0, concat_axis=0, tiled=True)]
    dynamic_update_slice x0 -> x15, local copies, waits for them, and re-layouts: none -> 11.8 us  [state_cards_on_mesh(): lax.dynamic_update_slice_in_dim(wide_out, arr_out, (new ^ num) * field_ou...]
  transfers between devices with their start and end apart: 9 -> 23, of which waited for: 8 -> 18; matrix products, arithmetic and copies ran while one was open for 19% -> 15% of each run, Pallas kernels for 0% -> 0%
where the time goes in v1:
time: 817 us; the launch traced here: 802 us
  waiting for transfers between devices  427 us (52%)
  local copies, waits for them, and re-layouts  165 us (20%)
  starting transfers between devices  70.9 us (9%)
  other arithmetic  67.5 us (8%)
  matrix products  56.2 us (7%)
  between operations  14.6 us (2%)
    ppermute x15, waiting for transfers between devices, state_cards_on_mesh(): lax.ppermute(arr_out, axis_name='req', perm=list(map(lambda k: (k, k ^ nu...  207 us
    all_to_all x1, waiting for transfers between devices, body(): lax.all_to_all(buffer, 'req', split_axis=0, concat_axis=0, tiled=True)  176 us
    sub x2, other arithmetic, soft_weights(): probability = jnp.where(allowed, jnp.exp(masked - row_max), 0.0)  38.7 us
    scatter x1, local copies, waits for them, and re-layouts, body(): decode_pool = jnp.zeros((slots_dev, group_count, BLOCK, head_pair), jnp.b...  33.5 us
    scatter x1, local copies, waits for them, and re-layouts, body(): buffer = jnp.zeros((experts * capacity, width_model), jnp.bfloat16).at[ta...  33.3 us
    all_to_all x1, waiting for transfers between devices, body(): lax.all_to_all(cache, 'kv', split_axis=2, concat_axis=1, tiled=True)  32.6 us
    ppermute x15, starting transfers between devices, state_cards_on_mesh(): lax.ppermute(arr_out, axis_name='req', perm=list(map(lambda k: (k, k ^ nu...  32.2 us
    dynamic_slice x10, local copies, waits for them, and re-layouts, body(): lax.map(whole_request, (query_heads, cache_heads, span_heads, lengths))  18.9 us
  transfers between devices with their start and end apart: 23, of which 18 were waited for; matrix products, arithmetic and copies ran while one was open for 15% of the time, Pallas kernels for 0%

profile of v1, /device:TPU:11, one launch (start us, length us, event | category | flops | bytes accessed | tf_op | source)
XLA Modules:
  0.0 802.1 jit_solution(10293400919820019693)
XLA Ops:
  9.3 3.5 all-to-all-start.1
  14.9 5.2 all-to-all-done.1
  20.1 3.5 all-to-all-start.2
  23.6 5.0 copy.78
  30.1 5.6 all-to-all-start
  36.9 4.5 reduce-window.6
  48.0 32.6 %all-to-all-done = bf16[2,1024,8,128]{3,1,0,2:T(8,128)(2,1)} async-done(((bf16[2,1024,8,128]{3,1,0,2:T(8,128)(2,1)}), bf16[2,1024,8,128]{3,1,0,2:T(8,128)(2,1)}, u32[]{:S(2)}, u32[]{:S(2)}) %all-to-all-start) | async-done | bytes 4194336 | tf_op jit(solution)/shard_map/all_to_all | solution.py:112
  80.6 4.6 copy.80
  85.2 99.9 %while.12 = (s32[]{:T(128)}, bf16[2,256,4,128]{3,2,0,1:T(4,128)(2,1)}, bf16[2,2048,4,128]{3,1,2,0:T(8,128)(2,1)}, bf16[2,256,4,128]{1,3,2,0:T(8,128)(2,1)}, s32[...) while((s32[]{:T(128)}, bf16[2,256,4,128]{3,2,0,1:T(4,128)(2,1)}, ...), condition=%wide.region_4.5_spmd, body=%wide.region_1.4_spmd.sunk | while | flops 1251877888 | bytes 76983440 | solution.py:116
  88.0 3.1 constant_dynamic-slice_fusion.20
  91.1 4.0 copy.115
  96.8 7.9 fusion.65
  109.4 19.4 %fusion.67 = (f32[4,2,256]{2,1,0:T(2,128)S(1)}, bf16[4,2,256,2304]{2,3,1,0:T(8,128)(2,1)}) fusion(f32[4,2304,256,2]{2,1,3,0:T(8,128)} %fusion.65, pred[256,2304]{0,1:T(8,128)(4,1)} %fusion.66), kind=kOutput, calls=%fused_computation.130.clone.1 | output fusion | flops 37751040 | bytes 28909568 | tf_op jit(solution)/shard_map/while/body/eval_jaxpr/sub | solution.py:57
  128.8 5.4 fusion.68
  141.0 4.0 copy.115
  146.8 7.9 fusion.65
  159.4 19.4 %fusion.67 = (f32[4,2,256]{2,1,0:T(2,128)S(1)}, bf16[4,2,256,2304]{2,3,1,0:T(8,128)(2,1)}) fusion(f32[4,2304,256,2]{2,1,3,0:T(8,128)} %fusion.65, pred[256,2304]{0,1:T(8,128)(4,1)} %fusion.66), kind=kOutput, calls=%fused_computation.130.clone.1 | output fusion | flops 37751040 | bytes 28909568 | tf_op jit(solution)/shard_map/while/body/eval_jaxpr/sub | solution.py:57
  178.7 5.4 fusion.68
  185.2 4.1 all-to-all-start.3
  190.0 4.7 all-to-all-done.3
  199.0 33.3 %scatter_custom_fusion = bf16[4096,1024]{1,0:T(8,128)(2,1)} fusion(s32[2048]{0:T(1024)S(1)} %bitcast.205, bf16[256,1024]{1,0:T(8,128)(2,1)} %multiply_convert_fusion, s32[2048]{0:T(1024)S(1)} %broadcast_clamp_fusion.1, bf16[]{:T(256)} %constant.129.clone.1), kind=kCustom, calls=%fused_computation.49 | custom fusion | bytes 8389120 | tf_op jit(solution)/shard_map/scatter | solution.py:159
  232.3 10.6 %all-to-all-start.4 = ((bf16[16,256,1024]{2,1,0:T(8,128)(2,1)}), bf16[16,256,1024]{2,1,0:T(8,128)(2,1)}, u32[]{:S(2)}, u32[]{:S(2)}) async-start(bf16[16,256,1024]{2,1,0:T(8,128)(2,1)} %bitcast.189), calls=%async_computation.4 | async-start | bytes 16777216 | tf_op jit(solution)/shard_map/all_to_all | solution.py:163
  243.7 3.2 sort.17
  249.5 175.8 %all-to-all-done.4 = bf16[16,256,1024]{2,1,0:T(8,128)(2,1)} async-done(((bf16[16,256,1024]{2,1,0:T(8,128)(2,1)}), bf16[16,256,1024]{2,1,0:T(8,128)(2,1)}, u32[]{:S(2)}, u32[]{:S(2)}) %all-to-all-start.4) | async-done | bytes 8388640 | tf_op jit(solution)/shard_map/all_to_all | solution.py:163
  425.2 4.9 all-to-all-start.6
  430.2 11.4 %fusion.38 = f32[16,256,512]{2,1,0:T(8,128)} fusion(bf16[16,256,1024]{2,1,0:T(8,128)(2,1)} %all-to-all-done.4, bf16[1,3,1024,512]{3,2,1,0:T(8,128)(2,1)} %all-gather.2.cloned.1.call-done), kind=kOutput, calls=%fused_computation.58 | convolution fusion | flops 4294967296 | bytes 17825792 | tf_op jit(solution)/shard_map/sejd,edf->sejf/dot_general | solution.py:166
  441.5 16.0 %convolution_convert_fusion = bf16[16,256,1024]{2,1,0:T(8,128)(2,1)} fusion(f32[16,256,512]{2,1,0:T(8,128)} %fusion.38, bf16[16,256,1024]{2,1,0:T(8,128)(2,1)} %all-to-all-done.4, bf16[1,3,1024,512]{3,2,1,0:T(8,128)(2,1)} %all-gather.2.cloned.1.call-done), kind=kOutput, calls=%fused_computation.47 | convolution fusion | flops 8606711808 | bytes 27262976 | tf_op jit(solution)/shard_map/sejf,edf->sejd/dot_general | solution.py:173
  458.2 6.4 all-to-all-start.5
  468.0 3.3 copy.96
  471.3 5.2 gather_fusion.2
  491.6 24.6 %collective-permute-done.1 = bf16[1,16,4,16,128]{4,3,2,1,0:T(8,128)(2,1)S(1)} collective-permute-done((bf16[1,16,4,16,128]{4,3,2,1,0:T(8,128)(2,1)}, bf16[1,16,4,16,128]{4,3,2,1,0:T(8,128)(2,1)S(1)}, u32[]{:S(2)}, u32[]{:S(2)}) %collective-permute-start.1) | collective-permute-done | bytes 262176 | tf_op jit(solution)/shard_map/ppermute | solution.py:22
  516.3 3.4 collective-permute-start.6
  524.9 82.3 %collective-permute-done.3 = bf16[1,16,4,16,128]{4,3,2,1,0:T(8,128)(2,1)S(1)} collective-permute-done((bf16[1,16,4,16,128]{4,3,2,1,0:T(8,128)(2,1)}, bf16[1,16,4,16,128]{4,3,2,1,0:T(8,128)(2,1)S(1)}, u32[]{:S(2)}, u32[]{:S(2)}) %collective-permute-start.3) | collective-permute-done | bytes 262176 | tf_op jit(solution)/shard_map/ppermute | solution.py:22
  609.5 4.3 collective-permute-done.4
  614.5 3.1 collective-permute-done.5
  617.6 7.3 collective-permute-start.10
  625.6 6.2 collective-permute-start.11
  632.6 45.7 %collective-permute-done.7 = bf16[1,16,4,16,128]{4,3,2,1,0:T(8,128)(2,1)S(1)} collective-permute-done((bf16[1,16,4,16,128]{4,3,2,1,0:T(8,128)(2,1)}, bf16[1,16,4,16,128]{4,3,2,1,0:T(8,128)(2,1)S(1)}, u32[]{:S(2)}, u32[]{:S(2)}) %collective-permute-start.7) | collective-permute-done | bytes 262176 | tf_op jit(solution)/shard_map/ppermute | solution.py:22
  687.0 8.1 %collective-permute-done.9 = bf16[1,16,4,16,128]{4,3,2,1,0:T(8,128)(2,1)S(1)} collective-permute-done((bf16[1,16,4,16,128]{4,3,2,1,0:T(8,128)(2,1)}, bf16[1,16,4,16,128]{4,3,2,1,0:T(8,128)(2,1)S(1)}, u32[]{:S(2)}, u32[]{:S(2)}) %collective-permute-start.9) | collective-permute-done | bytes 262176 | tf_op jit(solution)/shard_map/ppermute | solution.py:22
  698.3 13.6 %collective-permute-done.10 = bf16[1,16,4,16,128]{4,3,2,1,0:T(8,128)(2,1)S(1)} collective-permute-done((bf16[1,16,4,16,128]{4,3,2,1,0:T(8,128)(2,1)}, bf16[1,16,4,16,128]{4,3,2,1,0:T(8,128)(2,1)S(1)}, u32[]{:S(2)}, u32[]{:S(2)}) %collective-permute-start.10) | collective-permute-done | bytes 262176 | tf_op jit(solution)/shard_map/ppermute | solution.py:22
  712.7 6.9 collective-permute-done.11
  720.2 5.8 collective-permute-done.12
  726.8 3.9 collective-permute-done.13
  731.5 5.1 collective-permute-done.14
  737.2 3.1 broadcast_in_dim.109
  740.3 33.5 %scatter_fusion = bf16[256,4,16,128]{3,2,1,0:T(8,128)(2,1)} fusion(bf16[256,4,16,128]{3,2,1,0:T(8,128)(2,1)} %broadcast_in_dim.109, s32[256]{0:T(256)S(1)} %bitcast.208, bf16[256,4,16,128]{3,2,1,0:T(8,128)(2,1)} %bitcast.57), kind=kCustom, calls=%fused_computation.5 | custom fusion | bytes 12583936 | tf_op jit(solution)/shard_map/scatter | solution.py:140
  773.8 15.4 %gather_fusion = bf16[2048,1024]{1,0:T(8,128)(2,1)} fusion(bf16[4096,1024]{1,0:T(8,128)(2,1)} %bitcast.46, s32[2048]{0:T(1024)S(1)} %broadcast_clamp_fusion), kind=kCustom, calls=%fused_computation.1 | custom fusion | bytes 8396800 | tf_op jit(solution)/shard_map/gather | solution.py:179
  789.2 4.8 fusion.26
  (129 shorter events, 90.4 us)
Async XLA Ops:
  7.2 188.9 %copy-start = (bf16[1024,1024]{1,0:T(8,128)(2,1)S(1)}, bf16[1024,1024]{1,0:T(8,128)(2,1)}, u32[]{:S(2)}) copy-start(bf16[1024,1024]{1,0:T(8,128)(2,1)} %param.20) | copy-start | bytes 6291460
  9.3 10.9 %all-to-all-start.1 = ((bf16[2,128,8,128]{3,1,0,2:T(8,128)(2,1)}), bf16[2,128,8,128]{3,1,0,2:T(8,128)(2,1)S(1)}, u32[]{:S(2)}, u32[]{:S(2)}) async-start(bf16[2,128,8,128]{3,1,0,2:T(8,128)(2,1)} %copy.81), calls=%async_computation.1 | async-start | bytes 1048576 | tf_op jit(solution)/shard_map/all_to_all | solution.py:113
  20.1 9.9 %all-to-all-start.2 = ((bf16[2,128,8,128]{1,3,0,2:T(8,128)(2,1)}), bf16[2,128,8,128]{1,3,0,2:T(8,128)(2,1)S(1)}, u32[]{:S(2)}, u32[]{:S(2)}) async-start(bf16[2,128,8,128]{1,3,0,2:T(8,128)(2,1)} %copy.84), calls=%async_computation.2 | async-start | bytes 1048576 | tf_op jit(solution)/shard_map/all_to_all | solution.py:114
  28.6 7.1 copy-start.4
  28.6 13.4 %copy-start.9 = (s32[32]{0:T(128)S(1)}, s32[32]{0:T(128)}, u32[]{:S(2)}) copy-start(s32[32]{0:T(128)} %param.18) | copy-start | bytes 388
  28.6 13.5 %copy-start.10 = (s32[32]{0:T(128)S(1)}, s32[32]{0:T(128)}, u32[]{:S(2)}) copy-start(s32[32]{0:T(128)} %param.19) | copy-start | bytes 388
  30.1 50.6 %all-to-all-start = ((bf16[2,1024,8,128]{3,1,0,2:T(8,128)(2,1)}), bf16[2,1024,8,128]{3,1,0,2:T(8,128)(2,1)}, u32[]{:S(2)}, u32[]{:S(2)}) async-start(bf16[2,1024,8,128]{3,1,0,2:T(8,128)(2,1)} %copy.78), calls=%async_computation | async-start | bytes 8388608 | tf_op jit(solution)/shard_map/all_to_all | solution.py:112
  85.2 104.0 %copy-start.6 = (s32[2048,1]{0,1:T(1,128)S(1)}, s32[2048,1]{0,1:T(1,128)}, u32[]{:S(2)}) copy-start(s32[2048,1]{0,1:T(1,128)} %mul.65) | copy-start | bytes 24580
  95.1 1.8 copy-start.2
  145.0 1.8 copy-start.2
  185.2 12.9 %copy-start.7 = (f32[1024]{0:T(1024)S(1)}, f32[1024]{0:T(1024)}, u32[]{:S(2)}) copy-start(f32[1024]{0:T(1024)} %param.21) | copy-start | bytes 12292
  185.2 9.5 %all-to-all-start.3 = ((bf16[2,256,4,128]{3,2,0,1:T(4,128)(2,1)}), bf16[2,256,4,128]{3,2,0,1:T(4,128)(2,1)S(1)}, u32[]{:S(2)}, u32[]{:S(2)}) async-start(bf16[2,256,4,128]{3,2,0,1:T(4,128)(2,1)} %get-tuple-element.80), calls=%async_computation.3 | async-start | bytes 1048576 | tf_op jit(solution)/shard_map/all_to_all | solution.py:117
  232.3 11.3 %copy-start.8 = (s32[2,128]{1,0:T(2,128)S(1)}, s32[2,128]{1,0:T(2,128)}, u32[]{:S(2)}) copy-start(s32[2,128]{1,0:T(2,128)} %param.25) | copy-start | bytes 3076
  232.3 192.9 %all-to-all-start.4 = ((bf16[16,256,1024]{2,1,0:T(8,128)(2,1)}), bf16[16,256,1024]{2,1,0:T(8,128)(2,1)}, u32[]{:S(2)}, u32[]{:S(2)}) async-start(bf16[16,256,1024]{2,1,0:T(8,128)(2,1)} %bitcast.189), calls=%async_computation.4 | async-start | bytes 16777216 | tf_op jit(solution)/shard_map/all_to_all | solution.py:163
  242.9 187.3 %all-gather.2.cloned.1.call-start = ((), (), s32[]{:S(2)}) async-start(), calls=%async_computation.7 | async-start | bytes 4718592 | tf_op jit(solution)/shard_map/all_gather | solution.py:162
  425.2 32.3 %all-to-all-start.6 = ((s32[16,1,16]{2,1,0:T(1,128)}), s32[16,1,16]{2,1,0:T(1,128)S(1)}, u32[]{:S(2)}, u32[]{:S(2)}) async-start(s32[16,1,16]{2,1,0:T(1,128)} %all_to_all.81), calls=%async_computation.6 | async-start | bytes 16384 | tf_op jit(solution)/shard_map/all_to_all | solution.py:133
  457.6 0.6 copy-start.5
  458.2 315.7 %all-to-all-start.5 = ((bf16[16,256,1024]{2,1,0:T(8,128)(2,1)}), bf16[16,256,1024]{2,1,0:T(8,128)(2,1)}, u32[]{:S(2)}, u32[]{:S(2)}) async-start(bf16[16,256,1024]{2,1,0:T(8,128)(2,1)} %convolution_convert_fusion), calls=%async_computation.5 | async-start | bytes 16777216 | tf_op jit(solution)/shard_map/all_to_all | solution.py:176
  476.5 3.0 copy-start.1
  482.0 7.9 collective-permute-start
  486.3 197.4 %copy-start.3 = (bf16[1,16,4,16,128]{4,3,2,1,0:T(8,128)(2,1)S(1)}, bf16[1,16,4,16,128]{4,3,2,1,0:T(8,128)(2,1)}, u32[]{:S(2)}) copy-start(bf16[1,16,4,16,128]{4,3,2,1,0:T(8,128)(2,1)} %get-tuple-element.133) | copy-start | bytes 786436
  486.3 29.9 %collective-permute-start.1 = (bf16[1,16,4,16,128]{4,3,2,1,0:T(8,128)(2,1)}, bf16[1,16,4,16,128]{4,3,2,1,0:T(8,128)(2,1)S(1)}, u32[]{:S(2)}, u32[]{:S(2)}) collective-permute-start(bf16[1,16,4,16,128]{4,3,2,1,0:T(8,128)(2,1)} %get-tuple-element.145), channel_id=1, source_target_pairs={{0,4},{2,6},{4,0},{6,2},{8,12},{10,14},{12,8},{14,10},{16,20},{18,... | collective-permute-start | bytes 786440 | tf_op jit(solution)/shard_map/ppermute | solution.py:22
  486.7 35.4 %collective-permute-start.2 = (bf16[1,16,4,16,128]{4,3,2,1,0:T(8,128)(2,1)}, bf16[1,16,4,16,128]{4,3,2,1,0:T(8,128)(2,1)S(1)}, u32[]{:S(2)}, u32[]{:S(2)}) collective-permute-start(bf16[1,16,4,16,128]{4,3,2,1,0:T(8,128)(2,1)} %get-tuple-element.144), channel_id=1, source_target_pairs={{0,6},{2,4},{4,2},{6,0},{8,14},{10,12},{12,10},{14,8},{16,22},{18,... | collective-permute-start | bytes 786440 | tf_op jit(solution)/shard_map/ppermute | solution.py:22
  488.2 119.1 %collective-permute-start.3 = (bf16[1,16,4,16,128]{4,3,2,1,0:T(8,128)(2,1)}, bf16[1,16,4,16,128]{4,3,2,1,0:T(8,128)(2,1)S(1)}, u32[]{:S(2)}, u32[]{:S(2)}) collective-permute-start(bf16[1,16,4,16,128]{4,3,2,1,0:T(8,128)(2,1)} %get-tuple-element.143), channel_id=1, source_target_pairs={{0,8},{2,10},{4,12},{6,14},{8,0},{10,2},{12,4},{14,6},{16,24},{18,... | collective-permute-start | bytes 786440 | tf_op jit(solution)/shard_map/ppermute | solution.py:22
  488.5 125.3 %collective-permute-start.4 = (bf16[1,16,4,16,128]{4,3,2,1,0:T(8,128)(2,1)}, bf16[1,16,4,16,128]{4,3,2,1,0:T(8,128)(2,1)S(1)}, u32[]{:S(2)}, u32[]{:S(2)}) collective-permute-start(bf16[1,16,4,16,128]{4,3,2,1,0:T(8,128)(2,1)} %get-tuple-element.142), channel_id=1, source_target_pairs={{0,10},{2,8},{4,14},{6,12},{8,2},{10,0},{12,6},{14,4},{16,26},{18,... | collective-permute-start | bytes 786440 | tf_op jit(solution)/shard_map/ppermute | solution.py:22
  489.9 127.7 %collective-permute-start.5 = (bf16[1,16,4,16,128]{4,3,2,1,0:T(8,128)(2,1)}, bf16[1,16,4,16,128]{4,3,2,1,0:T(8,128)(2,1)S(1)}, u32[]{:S(2)}, u32[]{:S(2)}) collective-permute-start(bf16[1,16,4,16,128]{4,3,2,1,0:T(8,128)(2,1)} %get-tuple-element.141), channel_id=1, source_target_pairs={{0,12},{2,14},{4,8},{6,10},{8,4},{10,6},{12,0},{14,2},{16,28},{18,... | collective-permute-start | bytes 786440 | tf_op jit(solution)/shard_map/ppermute | solution.py:22
  516.3 109.4 %collective-permute-start.6 = (bf16[1,16,4,16,128]{4,3,2,1,0:T(8,128)(2,1)}, bf16[1,16,4,16,128]{4,3,2,1,0:T(8,128)(2,1)S(1)}, u32[]{:S(2)}, u32[]{:S(2)}) collective-permute-start(bf16[1,16,4,16,128]{4,3,2,1,0:T(8,128)(2,1)} %get-tuple-element.140), channel_id=1, source_target_pairs={{0,14},{2,12},{4,10},{6,8},{8,6},{10,4},{12,2},{14,0},{16,30},{18,... | collective-permute-start | bytes 786440 | tf_op jit(solution)/shard_map/ppermute | solution.py:22
  522.1 156.2 %collective-permute-start.7 = (bf16[1,16,4,16,128]{4,3,2,1,0:T(8,128)(2,1)}, bf16[1,16,4,16,128]{4,3,2,1,0:T(8,128)(2,1)S(1)}, u32[]{:S(2)}, u32[]{:S(2)}) collective-permute-start(bf16[1,16,4,16,128]{4,3,2,1,0:T(8,128)(2,1)} %get-tuple-element.139), channel_id=1, source_target_pairs={{0,16},{2,18},{4,20},{6,22},{8,24},{10,26},{12,28},{14,30},{16,0},... | collective-permute-start | bytes 786440 | tf_op jit(solution)/shard_map/ppermute | solution.py:22
  607.3 76.5 %collective-permute-start.8 = (bf16[1,16,4,16,128]{4,3,2,1,0:T(8,128)(2,1)}, bf16[1,16,4,16,128]{4,3,2,1,0:T(8,128)(2,1)S(1)}, u32[]{:S(2)}, u32[]{:S(2)}) collective-permute-start(bf16[1,16,4,16,128]{4,3,2,1,0:T(8,128)(2,1)} %get-tuple-element.138), channel_id=1, source_target_pairs={{0,18},{2,16},{4,22},{6,20},{8,26},{10,24},{12,30},{14,28},{16,2},... | collective-permute-start | bytes 786440 | tf_op jit(solution)/shard_map/ppermute | solution.py:22
  613.8 81.3 %collective-permute-start.9 = (bf16[1,16,4,16,128]{4,3,2,1,0:T(8,128)(2,1)}, bf16[1,16,4,16,128]{4,3,2,1,0:T(8,128)(2,1)S(1)}, u32[]{:S(2)}, u32[]{:S(2)}) collective-permute-start(bf16[1,16,4,16,128]{4,3,2,1,0:T(8,128)(2,1)} %get-tuple-element.137), channel_id=1, source_target_pairs={{0,20},{2,22},{4,16},{6,18},{8,28},{10,30},{12,24},{14,26},{16,4},... | collective-permute-start | bytes 786440 | tf_op jit(solution)/shard_map/ppermute | solution.py:22
  617.6 94.3 %collective-permute-start.10 = (bf16[1,16,4,16,128]{4,3,2,1,0:T(8,128)(2,1)}, bf16[1,16,4,16,128]{4,3,2,1,0:T(8,128)(2,1)S(1)}, u32[]{:S(2)}, u32[]{:S(2)}) collective-permute-start(bf16[1,16,4,16,128]{4,3,2,1,0:T(8,128)(2,1)} %get-tuple-element.136), channel_id=1, source_target_pairs={{0,22},{2,20},{4,18},{6,16},{8,30},{10,28},{12,26},{14,24},{16,6},... | collective-permute-start | bytes 786440 | tf_op jit(solution)/shard_map/ppermute | solution.py:22
  625.6 93.9 %collective-permute-start.11 = (bf16[1,16,4,16,128]{4,3,2,1,0:T(8,128)(2,1)}, bf16[1,16,4,16,128]{4,3,2,1,0:T(8,128)(2,1)S(1)}, u32[]{:S(2)}, u32[]{:S(2)}) collective-permute-start(bf16[1,16,4,16,128]{4,3,2,1,0:T(8,128)(2,1)} %get-tuple-element.135), channel_id=1, source_target_pairs={{0,24},{2,26},{4,28},{6,30},{8,16},{10,18},{12,20},{14,22},{16,8},... | collective-permute-start | bytes 786440 | tf_op jit(solution)/shard_map/ppermute | solution.py:22
  678.2 47.8 %collective-permute-start.12 = (bf16[1,16,4,16,128]{4,3,2,1,0:T(8,128)(2,1)}, bf16[1,16,4,16,128]{4,3,2,1,0:T(8,128)(2,1)S(1)}, u32[]{:S(2)}, u32[]{:S(2)}) collective-permute-start(bf16[1,16,4,16,128]{4,3,2,1,0:T(8,128)(2,1)} %get-tuple-element.134), channel_id=1, source_target_pairs={{0,26},{2,24},{4,30},{6,28},{8,18},{10,16},{12,22},{14,20},{16,10}... | collective-permute-start | bytes 786440 | tf_op jit(solution)/shard_map/ppermute | solution.py:22
  683.7 47.0 %collective-permute-start.13 = (bf16[1,16,4,16,128]{4,3,2,1,0:T(8,128)(2,1)S(1)}, bf16[1,16,4,16,128]{4,3,2,1,0:T(8,128)(2,1)S(1)}, u32[]{:S(2)}, u32[]{:S(2)}) collective-permute-start(bf16[1,16,4,16,128]{4,3,2,1,0:T(8,128)(2,1)S(1)} %copy-done.3), channel_id=1, source_target_pairs={{0,28},{2,30},{4,24},{6,26},{8,20},{10,22},{12,16},{14,18},{16,12}... | collective-permute-start | bytes 786440 | tf_op jit(solution)/shard_map/ppermute | solution.py:22
  695.1 41.4 %collective-permute-start.14 = (bf16[1,16,4,16,128]{4,3,2,1,0:T(8,128)(2,1)S(1)}, bf16[1,16,4,16,128]{4,3,2,1,0:T(8,128)(2,1)S(1)}, u32[]{:S(2)}, u32[]{:S(2)}) collective-permute-start(bf16[1,16,4,16,128]{4,3,2,1,0:T(8,128)(2,1)S(1)} %get-tuple-element.132), channel_id=1, source_target_pairs={{0,30},{2,28},{4,26},{6,24},{8,22},{10,20},{12,18},{14,16},{16,14}... | collective-permute-start | bytes 786440 | tf_op jit(solution)/shard_map/ppermute | solution.py:22
Sparse Core Ops, SparseCore 0:
  245.3 44.5 all-gather.1
